TPU v7x, 32 devices: a whole 2x2x4 slice. The times are simulated.
32 devices in a mesh: groups: 2 (over y), dp: 4 (over z), task: 4 (over x, core).
Axes of the slice: x: 2, y: 2, z: 4, core: 2. Of those that a mesh axis runs over, the one named last changes fastest.
Arguments:
- coords: bfloat16 [3, 6144], P(None, ('groups', 'dp')), parts along dimension 1, may hold values from 0 to 1
- lengthscales: float32 [6], P('groups'), parts along dimension 0, may hold values from 0.15 to 0.5
- vectors: bfloat16 [2, 6144, 256], P(None, ('groups', 'dp'), 'task'), parts along dimension 1, may hold values from -6 to 6
- mixing: bfloat16 [512, 256], P('groups'), parts along dimension 0, may hold values from -0.078125 to 0.078125
- noise: float32 [512], P(('groups', 'task')), parts along dimension 0, may hold values from 0.1 to 1
Outputs:
- product: bfloat16 [2, 6144, 256], P(None, ('groups', 'dp'), 'task'), parts along dimension 1
- gradient: float32 [512, 256], P(('groups', 'task')), parts along dimension 0
There are 2 independent parts, one for each index of `groups`. A program takes and returns all parts, laid end to end along the dimension named above; each array names one. Nothing has to cross between parts.
All inputs are finite; a program needn't handle non-finite values.
Results may differ from a plain program's by a relative error of at most 0.0056.
Values may be sent and summed in bfloat16 or wider, within the bound.
No kernel may reach another device: no remote copies, remote signals or barrier semaphores. Data moves between devices by JAX's collectives and lax.ppermute only.
A program may use at most 64 MiB of HBM per device.

v0:
```python
import jax
import jax.numpy as jnp
from jax import lax
from jax.sharding import PartitionSpec as P


def kernel_tile(left, right):
    diff = left[:, :, None] - right[:, None, :]
    return jnp.exp(0.1 - jnp.sqrt(jnp.sum(diff * diff, axis=0) + 0.01))


def shift(x, axis, k, n):
    return lax.ppermute(x, axis, [(i, (i + k) % n) for i in range(n)])


def sum_over(x, axis, n):
    if n == 4:
        got = [shift(x, axis, k, n) for k in range(1, n)]
        even = lax.axis_index(axis) % 2 == 0
        first = x + jnp.where(even, got[2], got[0])
        second = got[1] + jnp.where(even, got[0], got[2])
        return first + second
    if n & n - 1:
        return lax.psum(x, axis)
    step = 1
    while step < n:
        x = x + lax.ppermute(x, axis, [(i, i ^ step) for i in range(n)])
        step *= 2
    return x


def per_device(coords, lengthscales, vectors, mixing, noise):
    n_rows = coords.shape[1]
    local_tasks = vectors.shape[2]
    n_dp = lax.axis_size("dp")
    task_start = lax.axis_index("task") * local_tasks
    inverse = 1.0 / lengthscales
    own_scaled = coords.astype(jnp.float32) * inverse[:, None]

    def block(right_coords, values):
        right = right_coords.astype(jnp.float32) * inverse[:, None]
        tile = kernel_tile(own_scaled, right).astype(jnp.bfloat16)
        return jnp.einsum("nr,srm->snm", tile, values, preferred_element_type=jnp.float32)

    task_input = vectors
    if n_dp <= 4:
        moved = [shift(vectors, "dp", k, n_dp) for k in range(1, n_dp)]
        if n_dp == 4:
            first = shift(coords, "dp", 1, n_dp)
            peer_coords = [first, shift(first, "dp", 1, n_dp), shift(coords, "dp", 3, n_dp)]
        else:
            peer_coords = [shift(coords, "dp", k, n_dp) for k in range(1, n_dp)]
        task_input = lax.optimization_barrier((vectors, peer_coords))[0]
        summed = block(coords, vectors)
        order = [1, 3, 2] if n_dp == 4 else list(range(1, n_dp))
        for k in order:
            summed = summed + block(peer_coords[k - 1], moved[k - 1])
    else:

        def ring(_, carry):
            accum, right_coords, values = carry
            right_coords = shift(right_coords, "dp", 1, n_dp)
            values = shift(values, "dp", 1, n_dp)
            return (accum + block(right_coords, values), right_coords, values)

        summed = block(coords, vectors)
        summed = lax.fori_loop(0, n_dp - 1, ring, (summed, coords, vectors))[0]
    n_task = lax.axis_size("task")
    copies = jnp.broadcast_to(task_input[None], (n_task,) + vectors.shape)
    task_blocks = lax.all_to_all(copies, "task", 0, 0, tiled=True)
    images = summed.astype(jnp.bfloat16)
    signs = jnp.array([1.0, -1.0], jnp.bfloat16)
    signed = images * signs[:, None, None]
    partial_grad = jnp.einsum(
        "sna,ksnb->akb", signed, task_blocks, preferred_element_type=jnp.float32
    ).reshape(local_tasks, n_task * local_tasks)
    total = sum_over(partial_grad, "dp", n_dp)
    gather_input = lax.optimization_barrier((images, task_blocks))[0]
    whole_images = lax.all_gather(
        jnp.transpose(gather_input, (2, 0, 1)), "task", axis=0, tiled=True
    )
    own_rows = lax.dynamic_slice_in_dim(mixing, task_start, local_tasks, 0)
    mixed = jnp.einsum("asn,ca->snc", whole_images, own_rows, preferred_element_type=jnp.float32)
    product = (mixed + noise[None, None, :] * vectors.astype(jnp.float32)).astype(jnp.bfloat16)
    gradient = total / (2.0 * n_rows * n_dp)
    return (product, gradient)


def solution(mesh):
    in_specs = (
        P(None, ("groups", "dp")),
        P("groups"),
        P(None, ("groups", "dp"), "task"),
        P("groups", None),
        P(("groups", "task")),
    )
    out_specs = (P(None, ("groups", "dp"), "task"), P(("groups", "task"), None))
    return jax.shard_map(
        per_device, mesh=mesh, in_specs=in_specs, out_specs=out_specs, check_vma=False
    )
```

profile of v0, /device:TPU:0, one launch (start us, length us, event | category | flops | bytes accessed | tf_op | source)
XLA Modules:
  0.0 54.8 jit_solution(17863950669732573691)
XLA Ops:
  0.6 0.0 copy-start
  0.6 0.0 copy-start.2
  0.7 3.1 %collective-permute-start = (bf16[3,768]{1,0:T(4,128)(2,1)}, bf16[3,768]{1,0:T(4,128)(2,1)S(1)}, u32[]{:S(2)}, u32[]{:S(2)}) collective-permute-start(bf16[3,768]{1,0:T(4,128)(2,1)} %param.6), channel_id=1, source_target_pairs={{0,4},{4,8},{8,12},{12,0},{1,5},{5,9},{9,13},{13,1},{2,6},{6,10},{... | collective-permute-start | bytes 13832 | tf_op jit(solution)/shard_map/ppermute | solution.py:13
  3.7 2.1 %collective-permute-start.2 = (bf16[3,768]{1,0:T(4,128)(2,1)}, bf16[3,768]{1,0:T(4,128)(2,1)S(1)}, u32[]{:S(2)}, u32[]{:S(2)}) collective-permute-start(bf16[3,768]{1,0:T(4,128)(2,1)} %param.6), channel_id=1, source_target_pairs={{0,12},{4,0},{8,4},{12,8},{1,13},{5,1},{9,5},{13,9},{2,14},{6,2},{... | collective-permute-start | bytes 13832 | tf_op jit(solution)/shard_map/ppermute | solution.py:13
  5.8 0.0 collective-permute-start.1
  5.8 3.8 %collective-permute-start.3 = (bf16[2,768,64]{1,2,0:T(8,128)(2,1)}, bf16[2,768,64]{1,2,0:T(8,128)(2,1)S(1)}, u32[]{:S(2)}, u32[]{:S(2)}) collective-permute-start(bf16[2,768,64]{1,2,0:T(8,128)(2,1)} %param.8), channel_id=1, source_target_pairs={{0,12},{4,0},{8,4},{12,8},{1,13},{5,1},{9,5},{13,9},{2,14},{6,2},{... | collective-permute-start | bytes 589832 | tf_op jit(solution)/shard_map/ppermute | solution.py:13
  9.6 0.0 collective-permute-start.5
  9.7 0.0 collective-permute-done
  9.7 0.7 %collective-permute-start.4 = (bf16[3,768]{1,0:T(4,128)(2,1)S(1)}, bf16[3,768]{1,0:T(4,128)(2,1)S(1)}, u32[]{:S(2)}, u32[]{:S(2)}) collective-permute-start(bf16[3,768]{1,0:T(4,128)(2,1)S(1)} %collective-permute-done), channel_id=1, source_target_pairs={{0,4},{4,8},{8,12},{12,0},{1,5},{5,9},{9,13},{13,1},{2,6},{6,10},{... | collective-permute-start | bytes 13832 | tf_op jit(solution)/shard_map/ppermute | solution.py:13
  10.4 0.7 %broadcast_divide_fusion = f32[3]{0:T(128)S(1)} fusion(f32[3]{0:T(128)} %param.7), kind=kLoop, calls=%fused_computation.28 | loop fusion | flops 3 | bytes 24 | tf_op jit(solution)/shard_map/div | solution.py:37
  11.0 0.0 collective-permute-done.2
  11.0 11.9 %collective-permute-done.4 = bf16[3,768]{1,0:T(4,128)(2,1)S(1)} collective-permute-done((bf16[3,768]{1,0:T(4,128)(2,1)S(1)}, bf16[3,768]{1,0:T(4,128)(2,1)S(1)}, u32[]{:S(2)}, u32[]{:S(2)}) %collective-permute-start.4) | collective-permute-done | bytes 4640 | tf_op jit(solution)/shard_map/ppermute | solution.py:13
  22.9 1.9 %broadcast_in_dim.2 = bf16[4,2,768,64]{2,3,1,0:T(8,128)(2,1)} broadcast(bf16[2,768,64]{1,2,0:T(8,128)(2,1)} %param.8), dimensions={1,2,3} | broadcast | bytes 983040 | tf_op jit(solution)/shard_map/broadcast_in_dim | solution.py:69
  24.8 3.5 %all-to-all-start = ((bf16[4,2,768,64]{2,3,1,0:T(8,128)(2,1)}), bf16[4,2,768,64]{2,3,1,0:T(8,128)(2,1)S(1)}, u32[]{:S(2)}, u32[]{:S(2)}) async-start(bf16[4,2,768,64]{2,3,1,0:T(8,128)(2,1)} %broadcast_in_dim.2), calls=%async_computation | async-start | bytes 1572864 | tf_op jit(solution)/shard_map/all_to_all | solution.py:70
  28.3 0.0 copy-done.2
  28.3 0.1 convert_multiply_fusion
  28.4 0.0 copy-start.1
  28.4 4.7 %multiply_reduce_fusion.2 = (f32[768,768]{1,0:T(8,128)S(1)}, f32[768,768]{1,0:T(8,128)S(1)}, f32[768,768]{1,0:T(8,128)S(1)}, f32[768,768]{1,0:T(8,128)S(1)}) fusion(f32[3,768]{1,0:T(4,128)S(1)} %get-tuple-element.11, f32[3,768]{1,0:T(4,128)S(1)} %get-tuple-element.13, f32[3,768]{1,0:T(4,128)S(1)} %get-tuple-element.12, f32[3,768]{1,0:T(4,128)S(1)} %get-tuple-element.10), kind=kLoop, calls=%fused_computation.2 | loop fusion | flops 18874368 | bytes 9474048 | tf_op jit(solution)/shard_map/reduce_sum | solution.py:9
  33.0 0.0 copy-done.1
  33.0 1.1 %fusion = f32[768,128]{0,1:S(1)} fusion(bf16[768,128]{0,1:T(8,128)(2,1)S(1)} %bitcast.35, f32[768,768]{1,0:T(8,128)S(1)} %get-tuple-element.9), kind=kOutput, calls=%fused_computation.9 | convolution fusion | flops 152764416 | bytes 2949120
  34.1 0.0 collective-permute-done.1
  34.1 1.1 %fusion.1 = f32[768,128]{0,1:S(1)} fusion(bf16[768,128]{0,1:T(8,128)(2,1)S(1)} %bitcast.42, f32[768,768]{1,0:T(8,128)S(1)} %get-tuple-element.6), kind=kOutput, calls=%fused_computation.10 | convolution fusion | flops 152764416 | bytes 2949120
  35.2 0.0 collective-permute-done.3
  35.2 1.1 %fusion.2 = f32[768,128]{0,1:S(1)} fusion(bf16[768,128]{0,1:T(8,128)(2,1)S(1)} %bitcast.41, f32[768,768]{1,0:T(8,128)S(1)} %get-tuple-element.7), kind=kOutput, calls=%fused_computation.11 | convolution fusion | flops 152764416 | bytes 2949120
  36.4 0.0 collective-permute-done.5
  36.4 0.0 copy-start.4
  36.4 1.1 %fusion.3 = f32[768,128]{0,1:S(1)} fusion(bf16[768,128]{0,1:T(8,128)(2,1)S(1)} %bitcast.40, f32[768,768]{1,0:T(8,128)S(1)} %get-tuple-element.8), kind=kOutput, calls=%fused_computation.12 | convolution fusion | flops 152764416 | bytes 2949120
  37.5 0.0 copy-start.3
  37.5 0.1 fusion.5
  37.6 2.3 %all-to-all-done = bf16[4,2,768,64]{2,3,1,0:T(8,128)(2,1)S(1)} async-done(((bf16[4,2,768,64]{2,3,1,0:T(8,128)(2,1)}), bf16[4,2,768,64]{2,3,1,0:T(8,128)(2,1)S(1)}, u32[]{:S(2)}, u32[]{:S(2)}) %all-to-all-start) | async-done | bytes 786464 | tf_op jit(solution)/shard_map/all_to_all | solution.py:70
  39.9 0.0 copy-done.4
  39.9 0.5 convolution_bitcast_fusion
  40.4 0.1 copy.9
  40.5 0.1 reshape.16
  40.6 0.0 collective-permute-start.6
  40.7 2.0 %collective-permute-start.7 = (f32[64,256]{1,0:T(8,128)S(1)}, f32[64,256]{1,0:T(8,128)S(1)}, u32[]{:S(2)}, u32[]{:S(2)}) collective-permute-start(f32[64,256]{1,0:T(8,128)S(1)} %reshape.16), channel_id=1, source_target_pairs={{0,4},{4,8},{8,12},{12,0},{1,5},{5,9},{9,13},{13,1},{2,6},{6,10},{... | collective-permute-start | bytes 196616 | tf_op jit(solution)/shard_map/ppermute | solution.py:13
  42.7 3.1 %collective-permute-start.8 = (f32[64,256]{1,0:T(8,128)S(1)}, f32[64,256]{1,0:T(8,128)S(1)}, u32[]{:S(2)}, u32[]{:S(2)}) collective-permute-start(f32[64,256]{1,0:T(8,128)S(1)} %reshape.16), channel_id=1, source_target_pairs={{0,8},{4,12},{8,0},{12,4},{1,9},{5,13},{9,1},{13,5},{2,10},{6,14},... | collective-permute-start | bytes 196616 | tf_op jit(solution)/shard_map/ppermute | solution.py:13
  45.8 7.4 %all_gather.3 = bf16[256,2,768]{2,0,1:T(8,128)(2,1)S(1)} all-gather(bf16[64,2,768]{2,0,1:T(8,128)(2,1)S(1)} %bitcast.34), channel_id=1, replica_groups=mesh['groups'=2,'dp'=4,'task'=4] {'task'}, dimensions={0}, use_global_device_ids=true | all-gather | bytes 983040 | tf_op jit(solution)/shard_map/all_gather | solution.py:79
  53.2 0.0 copy-done
  53.2 0.0 copy-done.3
  53.2 0.9 %fusion.4 = bf16[2,768,64]{1,2,0:T(8,128)(2,1)} fusion(bf16[256,2,768]{2,0,1:T(8,128)(2,1)S(1)} %all_gather.3, bf16[2,768,64]{1,2,0:T(8,128)(2,1)S(1)} %copy-done.1, f32[64]{0:T(128)S(1)} %copy-done.3, bf16[256,256]{1,0:T(8,128)(2,1)S(1)} %copy-done, s32[]{:T(128)S(6)} %select_n.22), kind=kOutput, calls=%fused_computation.13 | convolution fusion | flops 50724864 | bytes 1212932 | tf_op jit(solution)/shard_map/asn,ca->snc/dot_general | solution.py:83
  54.2 0.0 collective-permute-done.6
  54.2 0.0 collective-permute-done.7
  54.2 0.0 collective-permute-done.8
  54.2 0.7 %add_multiply_fusion = f32[64,256]{1,0:T(8,128)} fusion(f32[64,256]{1,0:T(8,128)S(1)} %collective-permute-done.8, f32[64,256]{1,0:T(8,128)S(1)} %collective-permute-done.7, f32[64,256]{1,0:T(8,128)S(1)} %collective-permute-done.6, f32[64,256]{1,0:T(8,128)S(1)} %reshape.16, pred[]{:T(512)S(6)} %eq.5), kind=kLoop, calls=%fused_computation.20 | loop fusion | flops 98304 | bytes 327681 | tf_op jit(solution)/shard_map/div | solution.py:85
Async XLA Ops:
  0.6 52.6 %copy-start = (bf16[256,256]{1,0:T(8,128)(2,1)S(1)}, bf16[256,256]{1,0:T(8,128)(2,1)}, u32[]{:S(2)}) copy-start(bf16[256,256]{1,0:T(8,128)(2,1)} %param.9) | copy-start | bytes 393220
  0.6 27.6 %copy-start.2 = (bf16[3,768]{1,0:T(4,128)(2,1)S(1)}, bf16[3,768]{1,0:T(4,128)(2,1)}, u32[]{:S(2)}) copy-start(bf16[3,768]{1,0:T(4,128)(2,1)} %param.6) | copy-start | bytes 13828
  0.7 9.0 %collective-permute-start = (bf16[3,768]{1,0:T(4,128)(2,1)}, bf16[3,768]{1,0:T(4,128)(2,1)S(1)}, u32[]{:S(2)}, u32[]{:S(2)}) collective-permute-start(bf16[3,768]{1,0:T(4,128)(2,1)} %param.6), channel_id=1, source_target_pairs={{0,4},{4,8},{8,12},{12,0},{1,5},{5,9},{9,13},{13,1},{2,6},{6,10},{... | collective-permute-start | bytes 13832 | tf_op jit(solution)/shard_map/ppermute | solution.py:13
  3.7 7.3 %collective-permute-start.2 = (bf16[3,768]{1,0:T(4,128)(2,1)}, bf16[3,768]{1,0:T(4,128)(2,1)S(1)}, u32[]{:S(2)}, u32[]{:S(2)}) collective-permute-start(bf16[3,768]{1,0:T(4,128)(2,1)} %param.6), channel_id=1, source_target_pairs={{0,12},{4,0},{8,4},{12,8},{1,13},{5,1},{9,5},{13,9},{2,14},{6,2},{... | collective-permute-start | bytes 13832 | tf_op jit(solution)/shard_map/ppermute | solution.py:13
  5.8 28.3 %collective-permute-start.1 = (bf16[2,768,64]{1,2,0:T(8,128)(2,1)}, bf16[2,768,64]{1,2,0:T(8,128)(2,1)S(1)}, u32[]{:S(2)}, u32[]{:S(2)}) collective-permute-start(bf16[2,768,64]{1,2,0:T(8,128)(2,1)} %param.8), channel_id=1, source_target_pairs={{0,4},{4,8},{8,12},{12,0},{1,5},{5,9},{9,13},{13,1},{2,6},{6,10},{... | collective-permute-start | bytes 589832 | tf_op jit(solution)/shard_map/ppermute | solution.py:13
  5.8 29.4 %collective-permute-start.3 = (bf16[2,768,64]{1,2,0:T(8,128)(2,1)}, bf16[2,768,64]{1,2,0:T(8,128)(2,1)S(1)}, u32[]{:S(2)}, u32[]{:S(2)}) collective-permute-start(bf16[2,768,64]{1,2,0:T(8,128)(2,1)} %param.8), channel_id=1, source_target_pairs={{0,12},{4,0},{8,4},{12,8},{1,13},{5,1},{9,5},{13,9},{2,14},{6,2},{... | collective-permute-start | bytes 589832 | tf_op jit(solution)/shard_map/ppermute | solution.py:13
  9.6 26.7 %collective-permute-start.5 = (bf16[2,768,64]{1,2,0:T(8,128)(2,1)}, bf16[2,768,64]{1,2,0:T(8,128)(2,1)S(1)}, u32[]{:S(2)}, u32[]{:S(2)}) collective-permute-start(bf16[2,768,64]{1,2,0:T(8,128)(2,1)} %param.8), channel_id=1, source_target_pairs={{0,8},{4,12},{8,0},{12,4},{1,9},{5,13},{9,1},{13,5},{2,10},{6,14},... | collective-permute-start | bytes 589832 | tf_op jit(solution)/shard_map/ppermute | solution.py:13
  9.7 13.2 %collective-permute-start.4 = (bf16[3,768]{1,0:T(4,128)(2,1)S(1)}, bf16[3,768]{1,0:T(4,128)(2,1)S(1)}, u32[]{:S(2)}, u32[]{:S(2)}) collective-permute-start(bf16[3,768]{1,0:T(4,128)(2,1)S(1)} %collective-permute-done), channel_id=1, source_target_pairs={{0,4},{4,8},{8,12},{12,0},{1,5},{5,9},{9,13},{13,1},{2,6},{6,10},{... | collective-permute-start | bytes 13832 | tf_op jit(solution)/shard_map/ppermute | solution.py:13
  24.8 15.1 %all-to-all-start = ((bf16[4,2,768,64]{2,3,1,0:T(8,128)(2,1)}), bf16[4,2,768,64]{2,3,1,0:T(8,128)(2,1)S(1)}, u32[]{:S(2)}, u32[]{:S(2)}) async-start(bf16[4,2,768,64]{2,3,1,0:T(8,128)(2,1)} %broadcast_in_dim.2), calls=%async_computation | async-start | bytes 1572864 | tf_op jit(solution)/shard_map/all_to_all | solution.py:70
  28.4 4.7 %copy-start.1 = (bf16[2,768,64]{1,2,0:T(8,128)(2,1)S(1)}, bf16[2,768,64]{1,2,0:T(8,128)(2,1)}, u32[]{:S(2)}) copy-start(bf16[2,768,64]{1,2,0:T(8,128)(2,1)} %param.8) | copy-start | bytes 589828
  36.4 3.5 %copy-start.4 = (bf16[2]{0:T(256)(128)(2,1)S(1)}, bf16[2]{0:T(256)(128)(2,1)}, u32[]{:S(2)}) copy-start(bf16[2]{0:T(256)(128)(2,1)} %constant.38.clone) | copy-start | bytes 16
  37.5 15.8 %copy-start.3 = (f32[64]{0:T(128)S(1)}, f32[64]{0:T(128)}, u32[]{:S(2)}) copy-start(f32[64]{0:T(128)} %param.10) | copy-start | bytes 772
  40.6 13.5 %collective-permute-start.6 = (f32[64,256]{1,0:T(8,128)S(1)}, f32[64,256]{1,0:T(8,128)S(1)}, u32[]{:S(2)}, u32[]{:S(2)}) collective-permute-start(f32[64,256]{1,0:T(8,128)S(1)} %reshape.16), channel_id=1, source_target_pairs={{0,12},{4,0},{8,4},{12,8},{1,13},{5,1},{9,5},{13,9},{2,14},{6,2},{... | collective-permute-start | bytes 196616 | tf_op jit(solution)/shard_map/ppermute | solution.py:13
  40.7 13.5 %collective-permute-start.7 = (f32[64,256]{1,0:T(8,128)S(1)}, f32[64,256]{1,0:T(8,128)S(1)}, u32[]{:S(2)}, u32[]{:S(2)}) collective-permute-start(f32[64,256]{1,0:T(8,128)S(1)} %reshape.16), channel_id=1, source_target_pairs={{0,4},{4,8},{8,12},{12,0},{1,5},{5,9},{9,13},{13,1},{2,6},{6,10},{... | collective-permute-start | bytes 196616 | tf_op jit(solution)/shard_map/ppermute | solution.py:13
  42.7 11.5 %collective-permute-start.8 = (f32[64,256]{1,0:T(8,128)S(1)}, f32[64,256]{1,0:T(8,128)S(1)}, u32[]{:S(2)}, u32[]{:S(2)}) collective-permute-start(f32[64,256]{1,0:T(8,128)S(1)} %reshape.16), channel_id=1, source_target_pairs={{0,8},{4,12},{8,0},{12,4},{1,9},{5,13},{9,1},{13,5},{2,10},{6,14},... | collective-permute-start | bytes 196616 | tf_op jit(solution)/shard_map/ppermute | solution.py:13
where the time goes:
time: 55.1 us; the launch traced here: 54.8 us
  starting transfers between devices  18.3 us (33%)
  waiting for transfers between devices  14.2 us (26%)
  blocking collectives  7.45 us (14%)
  other arithmetic  6.12 us (11%)
  matrix products  5.86 us (11%)
  local copies, waits for them, and re-layouts  2.13 us (4%)
  between operations  0.74 us (1%)
    ppermute x9, starting transfers between devices, shift(): return lax.ppermute(x, axis, [(i, (i + k) % n) for i in range(n)])  14.8 us
    ppermute x9, waiting for transfers between devices, shift(): return lax.ppermute(x, axis, [(i, (i + k) % n) for i in range(n)])  11.9 us
    all_gather x1, blocking collectives, per_device(): lax.all_gather(jnp.transpose(gather_input, (2, 0, 1)), 'task', axis=0, ti...  7.45 us
    reduce_sum x1, other arithmetic, kernel_tile(): return jnp.exp(0.1 - jnp.sqrt(jnp.sum(diff * diff, axis=0) + 0.01))  4.65 us
    unnamed x4, matrix products  4.41 us
    all_to_all x1, starting transfers between devices, per_device(): task_blocks = lax.all_to_all(copies, 'task', 0, 0, tiled=True)  3.49 us
    all_to_all x1, waiting for transfers between devices, per_device(): task_blocks = lax.all_to_all(copies, 'task', 0, 0, tiled=True)  2.32 us
    broadcast_in_dim x1, local copies, waits for them, and re-layouts, per_device(): copies = jnp.broadcast_to(task_input[None], (n_task,) + vectors.shape)  1.87 us
  transfers between devices with their start and end apart: 10, of which 2 were waited for; matrix products, arithmetic and copies ran while one was open for 23% of the time, Pallas kernels for 0%

commit v1 on v0

--- a/solution.py
+++ b/solution.py
@@ -2,6 +2,23 @@
 import jax.numpy as jnp
 from jax import lax
 from jax.sharding import PartitionSpec as P
+
+
+def laid_out(parts, dim):
+    parts = jnp.moveaxis(parts, 0, dim)
+    dims = parts.shape
+    return parts.reshape(*dims[:dim], dims[dim] * dims[dim + 1], *dims[dim + 2 :])
+
+
+def gather_around(x, axis, dim):
+    length = lax.axis_size(axis)
+    right = [(i, (i + 1) % length) for i in range(length)]
+    tiles = [x]
+    while len(tiles) < length:
+        tiles.append(lax.ppermute(tiles[-1], axis, right))
+    here = lax.axis_index(axis)
+    tiles = jnp.stack(tiles)[(here - jnp.arange(length)) % length]
+    return laid_out(tiles, dim)
 
 
 def kernel_tile(left, right):
@@ -76,9 +93,7 @@
     ).reshape(local_tasks, n_task * local_tasks)
     total = sum_over(partial_grad, "dp", n_dp)
     gather_input = lax.optimization_barrier((images, task_blocks))[0]
-    whole_images = lax.all_gather(
-        jnp.transpose(gather_input, (2, 0, 1)), "task", axis=0, tiled=True
-    )
+    whole_images = gather_around(jnp.transpose(gather_input, (2, 0, 1)), "task", 0)
     own_rows = lax.dynamic_slice_in_dim(mixing, task_start, local_tasks, 0)
     mixed = jnp.einsum("asn,ca->snc", whole_images, own_rows, preferred_element_type=jnp.float32)
     product = (mixed + noise[None, None, :] * vectors.astype(jnp.float32)).astype(jnp.bfloat16)

time: 55.1 us -> 58.9 us (1.069)
  waiting for transfers between devices: 14.2 us -> 23.7 us
  blocking collectives: 7.45 us -> 0 us
  starting transfers between devices: 18.3 us -> 19.3 us
  local copies, waits for them, and re-layouts: 2.13 us -> 2.77 us
    all_gather x1 -> x0, blocking collectives: 7.45 us -> none  [per_device(): lax.all_gather(jnp.transpose(gather_input, (2, 0, 1)), 'task', axis=0, ti...]
    ppermute x0 -> x3, waiting for transfers between devices: none -> 6.44 us  [gather_around(): tiles.append(lax.ppermute(tiles[-1], axis, right))]
    ppermute x9, waiting for transfers between devices: 11.9 us -> 14.9 us  [shift(): return lax.ppermute(x, axis, [(i, (i + k) % n) for i in range(n)])]
    ppermute x9, starting transfers between devices: 14.8 us -> 15.8 us  [shift(): return lax.ppermute(x, axis, [(i, (i + k) % n) for i in range(n)])]
    gather x0 -> x2, local copies, waits for them, and re-layouts: none -> 0.65 us  [gather_around(): tiles = jnp.stack(tiles)[(here - jnp.arange(length)) % length]]
  transfers between devices with their start and end apart: 10 -> 13, of which waited for: 2 -> 6; matrix products, arithmetic and copies ran while one was open for 23% -> 22% of each run, Pallas kernels for 0% -> 0%
where the time goes in v1:
time: 58.9 us; the launch traced here: 58.7 us
  waiting for transfers between devices  23.7 us (40%)
  starting transfers between devices  19.3 us (33%)
  other arithmetic  6.24 us (11%)
  matrix products  5.84 us (10%)
  local copies, waits for them, and re-layouts  2.77 us (5%)
  between operations  0.77 us (1%)
    ppermute x9, starting transfers between devices, shift(): return lax.ppermute(x, axis, [(i, (i + k) % n) for i in range(n)])  15.8 us
    ppermute x9, waiting for transfers between devices, shift(): return lax.ppermute(x, axis, [(i, (i + k) % n) for i in range(n)])  14.9 us
    ppermute x3, waiting for transfers between devices, gather_around(): tiles.append(lax.ppermute(tiles[-1], axis, right))  6.44 us
    reduce_sum x1, other arithmetic, kernel_tile(): return jnp.exp(0.1 - jnp.sqrt(jnp.sum(diff * diff, axis=0) + 0.01))  4.65 us
    unnamed x4, matrix products  4.38 us
    all_to_all x1, starting transfers between devices, per_device(): task_blocks = lax.all_to_all(copies, 'task', 0, 0, tiled=True)  3.49 us
    all_to_all x1, waiting for transfers between devices, per_device(): task_blocks = lax.all_to_all(copies, 'task', 0, 0, tiled=True)  2.36 us
    broadcast_in_dim x1, local copies, waits for them, and re-layouts, per_device(): copies = jnp.broadcast_to(task_input[None], (n_task,) + vectors.shape)  1.86 us
  transfers between devices with their start and end apart: 13, of which 6 were waited for; matrix products, arithmetic and copies ran while one was open for 22% of the time, Pallas kernels for 0%

profile of v1, /device:TPU:0, one launch (start us, length us, event | category | flops | bytes accessed | tf_op | source)
XLA Modules:
  0.0 58.7 jit_solution(10898211522993841011)
XLA Ops:
  0.6 0.0 copy-start
  0.6 0.0 copy-start.2
  0.7 3.1 %collective-permute-start = (bf16[3,768]{1,0:T(4,128)(2,1)}, bf16[3,768]{1,0:T(4,128)(2,1)S(1)}, u32[]{:S(2)}, u32[]{:S(2)}) collective-permute-start(bf16[3,768]{1,0:T(4,128)(2,1)} %param.6), channel_id=1, source_target_pairs={{0,4},{4,8},{8,12},{12,0},{1,5},{5,9},{9,13},{13,1},{2,6},{6,10},{... | collective-permute-start | bytes 13832 | tf_op jit(solution)/shard_map/ppermute | solution.py:30
  3.7 2.1 %collective-permute-start.2 = (bf16[3,768]{1,0:T(4,128)(2,1)}, bf16[3,768]{1,0:T(4,128)(2,1)S(1)}, u32[]{:S(2)}, u32[]{:S(2)}) collective-permute-start(bf16[3,768]{1,0:T(4,128)(2,1)} %param.6), channel_id=1, source_target_pairs={{0,12},{4,0},{8,4},{12,8},{1,13},{5,1},{9,5},{13,9},{2,14},{6,2},{... | collective-permute-start | bytes 13832 | tf_op jit(solution)/shard_map/ppermute | solution.py:30
  5.8 0.0 collective-permute-start.1
  5.8 3.8 %collective-permute-start.3 = (bf16[2,768,64]{1,2,0:T(8,128)(2,1)}, bf16[2,768,64]{1,2,0:T(8,128)(2,1)S(1)}, u32[]{:S(2)}, u32[]{:S(2)}) collective-permute-start(bf16[2,768,64]{1,2,0:T(8,128)(2,1)} %param.8), channel_id=1, source_target_pairs={{0,12},{4,0},{8,4},{12,8},{1,13},{5,1},{9,5},{13,9},{2,14},{6,2},{... | collective-permute-start | bytes 589832 | tf_op jit(solution)/shard_map/ppermute | solution.py:30
  9.6 0.0 collective-permute-start.5
  9.7 0.0 collective-permute-done
  9.7 0.7 %collective-permute-start.4 = (bf16[3,768]{1,0:T(4,128)(2,1)S(1)}, bf16[3,768]{1,0:T(4,128)(2,1)S(1)}, u32[]{:S(2)}, u32[]{:S(2)}) collective-permute-start(bf16[3,768]{1,0:T(4,128)(2,1)S(1)} %collective-permute-done), channel_id=1, source_target_pairs={{0,4},{4,8},{8,12},{12,0},{1,5},{5,9},{9,13},{13,1},{2,6},{6,10},{... | collective-permute-start | bytes 13832 | tf_op jit(solution)/shard_map/ppermute | solution.py:30
  10.4 0.7 %broadcast_divide_fusion = f32[3]{0:T(128)S(1)} fusion(f32[3]{0:T(128)} %param.7), kind=kLoop, calls=%fused_computation.37 | loop fusion | flops 3 | bytes 24 | tf_op jit(solution)/shard_map/div | solution.py:54
  11.0 0.0 collective-permute-done.2
  11.0 11.9 %collective-permute-done.4 = bf16[3,768]{1,0:T(4,128)(2,1)S(1)} collective-permute-done((bf16[3,768]{1,0:T(4,128)(2,1)S(1)}, bf16[3,768]{1,0:T(4,128)(2,1)S(1)}, u32[]{:S(2)}, u32[]{:S(2)}) %collective-permute-start.4) | collective-permute-done | bytes 4640 | tf_op jit(solution)/shard_map/ppermute | solution.py:30
  22.9 1.9 %broadcast_in_dim.2 = bf16[4,2,768,64]{2,3,1,0:T(8,128)(2,1)} broadcast(bf16[2,768,64]{1,2,0:T(8,128)(2,1)} %param.8), dimensions={1,2,3} | broadcast | bytes 983040 | tf_op jit(solution)/shard_map/broadcast_in_dim | solution.py:86
  24.8 3.5 %all-to-all-start = ((bf16[4,2,768,64]{2,3,1,0:T(8,128)(2,1)}), bf16[4,2,768,64]{2,3,1,0:T(8,128)(2,1)S(1)}, u32[]{:S(2)}, u32[]{:S(2)}) async-start(bf16[4,2,768,64]{2,3,1,0:T(8,128)(2,1)} %broadcast_in_dim.2), calls=%async_computation | async-start | bytes 1572864 | tf_op jit(solution)/shard_map/all_to_all | solution.py:87
  28.3 0.0 copy-done.2
  28.3 0.1 convert_multiply_fusion
  28.4 0.0 copy-start.1
  28.4 4.7 %multiply_reduce_fusion.2 = (f32[768,768]{1,0:T(8,128)S(1)}, f32[768,768]{1,0:T(8,128)S(1)}, f32[768,768]{1,0:T(8,128)S(1)}, f32[768,768]{1,0:T(8,128)S(1)}) fusion(f32[3,768]{1,0:T(4,128)S(1)} %get-tuple-element.11, f32[3,768]{1,0:T(4,128)S(1)} %get-tuple-element.13, f32[3,768]{1,0:T(4,128)S(1)} %get-tuple-element.12, f32[3,768]{1,0:T(4,128)S(1)} %get-tuple-element.10), kind=kLoop, calls=%fused_computation.3 | loop fusion | flops 18874368 | bytes 9474048 | tf_op jit(solution)/shard_map/reduce_sum | solution.py:26
  33.0 0.0 copy-done.1
  33.0 1.1 %fusion = f32[768,128]{0,1:S(1)} fusion(bf16[768,128]{0,1:T(8,128)(2,1)S(1)} %bitcast.45, f32[768,768]{1,0:T(8,128)S(1)} %get-tuple-element.9), kind=kOutput, calls=%fused_computation.10 | convolution fusion | flops 152764416 | bytes 2949120
  34.1 0.0 collective-permute-done.1
  34.1 1.1 %fusion.1 = f32[768,128]{0,1:S(1)} fusion(bf16[768,128]{0,1:T(8,128)(2,1)S(1)} %bitcast.55, f32[768,768]{1,0:T(8,128)S(1)} %get-tuple-element.6), kind=kOutput, calls=%fused_computation.11 | convolution fusion | flops 152764416 | bytes 2949120
  35.2 0.0 collective-permute-done.3
  35.2 1.1 %fusion.2 = f32[768,128]{0,1:S(1)} fusion(bf16[768,128]{0,1:T(8,128)(2,1)S(1)} %bitcast.54, f32[768,768]{1,0:T(8,128)S(1)} %get-tuple-element.7), kind=kOutput, calls=%fused_computation.12 | convolution fusion | flops 152764416 | bytes 2949120
  36.3 0.0 collective-permute-done.5
  36.3 0.0 copy-start.4
  36.3 1.1 %fusion.3 = f32[768,128]{0,1:S(1)} fusion(bf16[768,128]{0,1:T(8,128)(2,1)S(1)} %bitcast.53, f32[768,768]{1,0:T(8,128)S(1)} %get-tuple-element.8), kind=kOutput, calls=%fused_computation.13 | convolution fusion | flops 152764416 | bytes 2949120
  37.4 0.1 fusion.5
  37.5 2.4 %all-to-all-done = bf16[4,2,768,64]{2,3,1,0:T(8,128)(2,1)S(1)} async-done(((bf16[4,2,768,64]{2,3,1,0:T(8,128)(2,1)}), bf16[4,2,768,64]{2,3,1,0:T(8,128)(2,1)S(1)}, u32[]{:S(2)}, u32[]{:S(2)}) %all-to-all-start) | async-done | bytes 786464 | tf_op jit(solution)/shard_map/all_to_all | solution.py:87
  39.9 0.0 collective-permute-start.6
  39.9 5.1 %collective-permute-done.6 = bf16[64,2,768]{2,0,1:T(8,128)(2,1)S(1)} collective-permute-done((bf16[64,2,768]{2,0,1:T(8,128)(2,1)S(1)}, bf16[64,2,768]{2,0,1:T(8,128)(2,1)S(1)}, u32[]{:S(2)}, u32[]{:S(2)}) %collective-permute-start.6) | collective-permute-done | bytes 196640 | tf_op jit(solution)/shard_map/ppermute | solution.py:18
  45.0 0.0 collective-permute-start.7
  45.0 0.0 copy-done.4
  45.0 0.5 convolution_bitcast_fusion
  45.5 0.1 copy.11
  45.6 0.1 reshape.69
  45.7 1.2 %collective-permute-start.10 = (f32[64,256]{1,0:T(8,128)S(1)}, f32[64,256]{1,0:T(8,128)S(1)}, u32[]{:S(2)}, u32[]{:S(2)}) collective-permute-start(f32[64,256]{1,0:T(8,128)S(1)} %reshape.69), channel_id=1, source_target_pairs={{0,4},{4,8},{8,12},{12,0},{1,5},{5,9},{9,13},{13,1},{2,6},{6,10},{... | collective-permute-start | bytes 196616 | tf_op jit(solution)/shard_map/ppermute | solution.py:30
  47.0 2.0 %collective-permute-start.11 = (f32[64,256]{1,0:T(8,128)S(1)}, f32[64,256]{1,0:T(8,128)S(1)}, u32[]{:S(2)}, u32[]{:S(2)}) collective-permute-start(f32[64,256]{1,0:T(8,128)S(1)} %reshape.69), channel_id=1, source_target_pairs={{0,8},{4,12},{8,0},{12,4},{1,9},{5,13},{9,1},{13,5},{2,10},{6,14},... | collective-permute-start | bytes 196616 | tf_op jit(solution)/shard_map/ppermute | solution.py:30
  48.9 2.8 %collective-permute-start.9 = (f32[64,256]{1,0:T(8,128)S(1)}, f32[64,256]{1,0:T(8,128)S(1)}, u32[]{:S(2)}, u32[]{:S(2)}) collective-permute-start(f32[64,256]{1,0:T(8,128)S(1)} %reshape.69), channel_id=1, source_target_pairs={{0,12},{4,0},{8,4},{12,8},{1,13},{5,1},{9,5},{13,9},{2,14},{6,2},{... | collective-permute-start | bytes 196616 | tf_op jit(solution)/shard_map/ppermute | solution.py:30
  51.8 0.0 collective-permute-done.7
  51.8 0.1 collective-permute-start.8
  51.8 0.3 collective-permute-done.10
  52.2 2.7 %collective-permute-done.11 = f32[64,256]{1,0:T(8,128)S(1)} collective-permute-done((f32[64,256]{1,0:T(8,128)S(1)}, f32[64,256]{1,0:T(8,128)S(1)}, u32[]{:S(2)}, u32[]{:S(2)}) %collective-permute-start.11) | collective-permute-done | bytes 65568 | tf_op jit(solution)/shard_map/ppermute | solution.py:30
  54.9 0.0 collective-permute-done.9
  54.9 0.6 %add_multiply_fusion = f32[64,256]{1,0:T(8,128)} fusion(f32[64,256]{1,0:T(8,128)S(1)} %collective-permute-done.11, f32[64,256]{1,0:T(8,128)S(1)} %collective-permute-done.10, f32[64,256]{1,0:T(8,128)S(1)} %collective-permute-done.9, f32[64,256]{1,0:T(8,128)S(1)} %reshape.69, pred[]{:T(512)S(6)} %eq.7), kind=kLoop, calls=%fused_computation.22 | loop fusion | flops 98304 | bytes 327681 | tf_op jit(solution)/shard_map/div | solution.py:100
  55.6 1.4 %collective-permute-done.8 = bf16[64,2,768]{2,0,1:T(8,128)(2,1)S(1)} collective-permute-done((bf16[64,2,768]{2,0,1:T(8,128)(2,1)S(1)}, bf16[64,2,768]{2,0,1:T(8,128)(2,1)S(1)}, u32[]{:S(2)}, u32[]{:S(2)}) %collective-permute-start.8) | collective-permute-done | bytes 196640 | tf_op jit(solution)/shard_map/ppermute | solution.py:18
  56.9 0.0 copy-start.3
  56.9 0.1 pad_maximum_fusion
  57.0 0.6 %gather_fusion = bf16[4,64,2,768]{3,1,2,0:T(8,128)(2,1)S(1)} fusion(bf16[4,64,2,768]{3,1,2,0:T(8,128)(2,1)S(1)} %pad_maximum_fusion, s32[1024]{0:T(1024)S(1)} %pad_clamp_fusion), kind=kCustom, calls=%fused_computation | custom fusion | bytes 1572880 | tf_op jit(solution)/shard_map/gather | solution.py:20
  57.6 0.1 copy.10
  57.7 0.0 copy-done
  57.7 0.0 copy-done.3
  57.7 1.0 %fusion.4 = bf16[2,768,64]{1,2,0:T(8,128)(2,1)} fusion(bf16[256,2,768]{2,0,1:T(8,128)(2,1)S(1)} %bitcast.42, bf16[2,768,64]{1,2,0:T(8,128)(2,1)S(1)} %copy-done.1, f32[64]{0:T(128)S(1)} %copy-done.3, bf16[256,256]{1,0:T(8,128)(2,1)S(1)} %copy-done, s32[]{:T(128)S(6)} %select_n.47), kind=kOutput, calls=%fused_computation.14 | convolution fusion | flops 50724864 | bytes 1212932 | tf_op jit(solution)/shard_map/asn,ca->snc/dot_general | solution.py:98
  (2 shorter events, 0.0 us)
Async XLA Ops:
  0.6 57.1 %copy-start = (bf16[256,256]{1,0:T(8,128)(2,1)S(1)}, bf16[256,256]{1,0:T(8,128)(2,1)}, u32[]{:S(2)}) copy-start(bf16[256,256]{1,0:T(8,128)(2,1)} %param.9) | copy-start | bytes 393220
  0.6 27.6 %copy-start.2 = (bf16[3,768]{1,0:T(4,128)(2,1)S(1)}, bf16[3,768]{1,0:T(4,128)(2,1)}, u32[]{:S(2)}) copy-start(bf16[3,768]{1,0:T(4,128)(2,1)} %param.6) | copy-start | bytes 13828
  0.7 9.0 %collective-permute-start = (bf16[3,768]{1,0:T(4,128)(2,1)}, bf16[3,768]{1,0:T(4,128)(2,1)S(1)}, u32[]{:S(2)}, u32[]{:S(2)}) collective-permute-start(bf16[3,768]{1,0:T(4,128)(2,1)} %param.6), channel_id=1, source_target_pairs={{0,4},{4,8},{8,12},{12,0},{1,5},{5,9},{9,13},{13,1},{2,6},{6,10},{... | collective-permute-start | bytes 13832 | tf_op jit(solution)/shard_map/ppermute | solution.py:30
  3.7 7.3 %collective-permute-start.2 = (bf16[3,768]{1,0:T(4,128)(2,1)}, bf16[3,768]{1,0:T(4,128)(2,1)S(1)}, u32[]{:S(2)}, u32[]{:S(2)}) collective-permute-start(bf16[3,768]{1,0:T(4,128)(2,1)} %param.6), channel_id=1, source_target_pairs={{0,12},{4,0},{8,4},{12,8},{1,13},{5,1},{9,5},{13,9},{2,14},{6,2},{... | collective-permute-start | bytes 13832 | tf_op jit(solution)/shard_map/ppermute | solution.py:30
  5.8 28.3 %collective-permute-start.1 = (bf16[2,768,64]{1,2,0:T(8,128)(2,1)}, bf16[2,768,64]{1,2,0:T(8,128)(2,1)S(1)}, u32[]{:S(2)}, u32[]{:S(2)}) collective-permute-start(bf16[2,768,64]{1,2,0:T(8,128)(2,1)} %param.8), channel_id=1, source_target_pairs={{0,4},{4,8},{8,12},{12,0},{1,5},{5,9},{9,13},{13,1},{2,6},{6,10},{... | collective-permute-start | bytes 589832 | tf_op jit(solution)/shard_map/ppermute | solution.py:30
  5.8 29.4 %collective-permute-start.3 = (bf16[2,768,64]{1,2,0:T(8,128)(2,1)}, bf16[2,768,64]{1,2,0:T(8,128)(2,1)S(1)}, u32[]{:S(2)}, u32[]{:S(2)}) collective-permute-start(bf16[2,768,64]{1,2,0:T(8,128)(2,1)} %param.8), channel_id=1, source_target_pairs={{0,12},{4,0},{8,4},{12,8},{1,13},{5,1},{9,5},{13,9},{2,14},{6,2},{... | collective-permute-start | bytes 589832 | tf_op jit(solution)/shard_map/ppermute | solution.py:30
  9.6 26.7 %collective-permute-start.5 = (bf16[2,768,64]{1,2,0:T(8,128)(2,1)}, bf16[2,768,64]{1,2,0:T(8,128)(2,1)S(1)}, u32[]{:S(2)}, u32[]{:S(2)}) collective-permute-start(bf16[2,768,64]{1,2,0:T(8,128)(2,1)} %param.8), channel_id=1, source_target_pairs={{0,8},{4,12},{8,0},{12,4},{1,9},{5,13},{9,1},{13,5},{2,10},{6,14},... | collective-permute-start | bytes 589832 | tf_op jit(solution)/shard_map/ppermute | solution.py:30
  9.7 13.2 %collective-permute-start.4 = (bf16[3,768]{1,0:T(4,128)(2,1)S(1)}, bf16[3,768]{1,0:T(4,128)(2,1)S(1)}, u32[]{:S(2)}, u32[]{:S(2)}) collective-permute-start(bf16[3,768]{1,0:T(4,128)(2,1)S(1)} %collective-permute-done), channel_id=1, source_target_pairs={{0,4},{4,8},{8,12},{12,0},{1,5},{5,9},{9,13},{13,1},{2,6},{6,10},{... | collective-permute-start | bytes 13832 | tf_op jit(solution)/shard_map/ppermute | solution.py:30
  24.8 15.1 %all-to-all-start = ((bf16[4,2,768,64]{2,3,1,0:T(8,128)(2,1)}), bf16[4,2,768,64]{2,3,1,0:T(8,128)(2,1)S(1)}, u32[]{:S(2)}, u32[]{:S(2)}) async-start(bf16[4,2,768,64]{2,3,1,0:T(8,128)(2,1)} %broadcast_in_dim.2), calls=%async_computation | async-start | bytes 1572864 | tf_op jit(solution)/shard_map/all_to_all | solution.py:87
  28.4 4.7 %copy-start.1 = (bf16[2,768,64]{1,2,0:T(8,128)(2,1)S(1)}, bf16[2,768,64]{1,2,0:T(8,128)(2,1)}, u32[]{:S(2)}) copy-start(bf16[2,768,64]{1,2,0:T(8,128)(2,1)} %param.8) | copy-start | bytes 589828
  36.3 8.7 %copy-start.4 = (bf16[2]{0:T(256)(128)(2,1)S(1)}, bf16[2]{0:T(256)(128)(2,1)}, u32[]{:S(2)}) copy-start(bf16[2]{0:T(256)(128)(2,1)} %constant.54.clone) | copy-start | bytes 16
  39.9 5.1 %collective-permute-start.6 = (bf16[64,2,768]{2,0,1:T(8,128)(2,1)S(1)}, bf16[64,2,768]{2,0,1:T(8,128)(2,1)S(1)}, u32[]{:S(2)}, u32[]{:S(2)}) collective-permute-start(bf16[64,2,768]{2,0,1:T(8,128)(2,1)S(1)} %bitcast.43), channel_id=1, source_target_pairs={{0,1},{1,2},{2,3},{3,0},{4,5},{5,6},{6,7},{7,4},{8,9},{9,10},{10,1... | collective-permute-start | bytes 589832 | tf_op jit(solution)/shard_map/ppermute | solution.py:18
  45.0 6.8 %collective-permute-start.7 = (bf16[64,2,768]{2,0,1:T(8,128)(2,1)S(1)}, bf16[64,2,768]{2,0,1:T(8,128)(2,1)S(1)}, u32[]{:S(2)}, u32[]{:S(2)}) collective-permute-start(bf16[64,2,768]{2,0,1:T(8,128)(2,1)S(1)} %collective-permute-done.6), channel_id=1, source_target_pairs={{0,1},{1,2},{2,3},{3,0},{4,5},{5,6},{6,7},{7,4},{8,9},{9,10},{10,1... | collective-permute-start | bytes 589832 | tf_op jit(solution)/shard_map/ppermute | solution.py:18
  45.7 6.4 %collective-permute-start.10 = (f32[64,256]{1,0:T(8,128)S(1)}, f32[64,256]{1,0:T(8,128)S(1)}, u32[]{:S(2)}, u32[]{:S(2)}) collective-permute-start(f32[64,256]{1,0:T(8,128)S(1)} %reshape.69), channel_id=1, source_target_pairs={{0,4},{4,8},{8,12},{12,0},{1,5},{5,9},{9,13},{13,1},{2,6},{6,10},{... | collective-permute-start | bytes 196616 | tf_op jit(solution)/shard_map/ppermute | solution.py:30
  47.0 8.0 %collective-permute-start.11 = (f32[64,256]{1,0:T(8,128)S(1)}, f32[64,256]{1,0:T(8,128)S(1)}, u32[]{:S(2)}, u32[]{:S(2)}) collective-permute-start(f32[64,256]{1,0:T(8,128)S(1)} %reshape.69), channel_id=1, source_target_pairs={{0,8},{4,12},{8,0},{12,4},{1,9},{5,13},{9,1},{13,5},{2,10},{6,14},... | collective-permute-start | bytes 196616 | tf_op jit(solution)/shard_map/ppermute | solution.py:30
  48.9 6.0 %collective-permute-start.9 = (f32[64,256]{1,0:T(8,128)S(1)}, f32[64,256]{1,0:T(8,128)S(1)}, u32[]{:S(2)}, u32[]{:S(2)}) collective-permute-start(f32[64,256]{1,0:T(8,128)S(1)} %reshape.69), channel_id=1, source_target_pairs={{0,12},{4,0},{8,4},{12,8},{1,13},{5,1},{9,5},{13,9},{2,14},{6,2},{... | collective-permute-start | bytes 196616 | tf_op jit(solution)/shard_map/ppermute | solution.py:30
  51.8 5.1 %collective-permute-start.8 = (bf16[64,2,768]{2,0,1:T(8,128)(2,1)S(1)}, bf16[64,2,768]{2,0,1:T(8,128)(2,1)S(1)}, u32[]{:S(2)}, u32[]{:S(2)}) collective-permute-start(bf16[64,2,768]{2,0,1:T(8,128)(2,1)S(1)} %collective-permute-done.7), channel_id=1, source_target_pairs={{0,1},{1,2},{2,3},{3,0},{4,5},{5,6},{6,7},{7,4},{8,9},{9,10},{10,1... | collective-permute-start | bytes 589832 | tf_op jit(solution)/shard_map/ppermute | solution.py:18
  56.9 0.8 %copy-start.3 = (f32[64]{0:T(128)S(1)}, f32[64]{0:T(128)}, u32[]{:S(2)}) copy-start(f32[64]{0:T(128)} %param.10) | copy-start | bytes 772
